TPU v7x, 32 devices: a whole 2x2x4 slice. The times are simulated.
32 devices in a mesh: grp: 8 (over z, y), band: 4 (over x, core).
Axes of the slice: x: 2, y: 2, z: 4, core: 2. Of those that a mesh axis runs over, the one named last changes fastest.
Arguments:
- x_blocks: bfloat16 [4, 4, 64, 8192], P('band', None, None, 'grp'), may hold values from -6 to 6
- pair_ids: int32 [8, 4, 4], P('grp', 'band'), may hold values from 0 to 15, as said below
- live_count: int32 [8, 4], P('grp', 'band'), may hold values from 2 to 4, as said below
- green_occ: bfloat16 [512, 512], replicated, may hold values from -0.0234375 to 0.0234375
- green_virt: bfloat16 [512, 512], replicated, may hold values from -0.0234375 to 0.0234375
Outputs:
- chi: float32 [128, 128], P(('grp', 'band'))
Inputs may be any that keep to these rules, and one draw needn't show every extreme that they name: On each device the 4 codes pair_ids[g, b, :] are distinct; code e names mu block e // 2 and nu block 2 * b + e % 2. `live_count`: in every draw some device has all 4 slots live.
All inputs are finite; a program needn't handle non-finite values.
Results may differ from a plain program's by a relative error of at most 0.0041.
Values may be sent and summed in bfloat16 or wider, within the bound.
No kernel may reach another device: no remote copies, remote signals or barrier semaphores. Data moves between devices by JAX's collectives and lax.ppermute only.
A program may use at most 128 MiB of HBM per device.

v0:
```python
import jax
import jax.numpy as jnp
from jax import lax
from jax.sharding import PartitionSpec as P


def on_device(x_blocks, pair_ids, live_count, green_occ, green_virt):
    local_blocks = x_blocks[0]
    pair_list = pair_ids[0, 0]
    live_slots = live_count[0, 0]
    slot_count = local_blocks.shape[0]
    block_size = local_blocks.shape[1]
    ri_cols = local_blocks.shape[2]
    ri_local = ri_cols // block_size
    orbitals = green_occ.shape[0]
    band_orbs = 2 * block_size
    band_count = lax.axis_size("band")
    group_count = lax.axis_size("grp")
    ri_total = ri_local * group_count
    mu_blocks = pair_list // 2
    half_codes = pair_list % 2
    slot_index = jnp.arange(slot_count, dtype=jnp.int32)
    row_index = (
        mu_blocks[:, None] * block_size + jnp.arange(block_size, dtype=jnp.int32)[None, :]
    ).reshape(-1)
    occ_rows = jnp.take(green_occ, row_index, axis=0).reshape(slot_count, block_size, orbitals)
    virt_rows = jnp.take(green_virt, row_index, axis=0).reshape(slot_count, block_size, orbitals)
    live_mask = slot_index < live_slots
    occ_halves = []
    virt_halves = []
    for half in range(2):
        weight = jnp.logical_and(live_mask, half_codes == half).astype(jnp.bfloat16)[:, None, None]
        occ_sel = occ_rows * weight
        virt_sel = virt_rows * weight
        occ_part = lax.dot_general(
            local_blocks, occ_sel, (((0, 1), (0, 1)), ((), ())), preferred_element_type=jnp.float32
        )
        virt_part = lax.dot_general(
            virt_sel, local_blocks, (((0, 1), (0, 1)), ((), ())), preferred_element_type=jnp.float32
        )
        occ_halves.append(occ_part.astype(jnp.bfloat16).reshape(ri_local, 1, block_size, orbitals))
        virt_halves.append(
            virt_part.astype(jnp.bfloat16).reshape(orbitals, ri_local, 1, block_size)
        )
    occ_three = jnp.concatenate(occ_halves, axis=1).reshape(ri_local, band_orbs, orbitals)
    virt_three = jnp.concatenate(virt_halves, axis=2).reshape(orbitals, ri_local, band_orbs)
    moved = lax.all_to_all(
        occ_three.reshape(ri_local, 1, band_orbs, band_count, band_orbs),
        "band",
        split_axis=3,
        concat_axis=1,
        tiled=True,
    )
    moved = moved.reshape(ri_local, orbitals, band_orbs)
    pair_cols = orbitals // group_count
    occ_pairs = lax.all_to_all(
        moved.reshape(ri_local, group_count, pair_cols, band_orbs),
        "grp",
        split_axis=1,
        concat_axis=0,
        tiled=True,
    )
    occ_pairs = occ_pairs.reshape(ri_total, pair_cols, band_orbs)
    virt_pairs = lax.all_to_all(
        virt_three.reshape(group_count, pair_cols, ri_local, band_orbs),
        "grp",
        split_axis=0,
        concat_axis=2,
        tiled=True,
    )
    virt_pairs = virt_pairs.reshape(pair_cols, ri_total, band_orbs)
    partial_value = lax.dot_general(
        occ_pairs, virt_pairs, (((1, 2), (0, 2)), ((), ())), preferred_element_type=jnp.float32
    )
    group_sum = lax.psum_scatter(partial_value, "grp", scatter_dimension=0, tiled=True)
    response = lax.psum_scatter(group_sum, "band", scatter_dimension=0, tiled=True)
    return response


def solution(mesh):
    placed = (P("band", None, None, "grp"), P("grp", "band", None), P("grp", "band"), P(), P())
    return jax.shard_map(
        on_device, mesh=mesh, in_specs=placed, out_specs=P(("grp", "band"), None), check_vma=False
    )
```

profile of v0, /device:TPU:0, one launch (start us, length us, event | category | flops | bytes accessed | tf_op | source)
XLA Modules:
  0.0 237.8 jit_solution(10687282440000746870)
XLA Ops:
  7.3 0.7 and_convert_fusion.1
  7.9 0.7 fusion.6
  8.8 2.3 gather_fusion
  11.1 1.2 gather_fusion.1
  12.8 0.5 fusion.1
  13.3 0.5 copy.16
  13.8 1.4 fusion
  15.2 1.5 copy.15
  17.2 2.1 reshape_reshape.9
  19.3 3.4 %copy.18 = bf16[16,1,128,4,128]{4,2,0,1,3:T(8,128)(2,1)} copy(bf16[16,1,128,4,128]{4,3,2,0,1:T(4,128)(2,1)} %reshape_reshape.9) | data formatting | bytes 4194304 | tf_op jit(solution)/shard_map/reshape;reshape | solution.py:48
  22.7 4.5 %all-to-all-start = ((bf16[16,1,128,4,128]{4,2,0,1,3:T(8,128)(2,1)}), bf16[16,1,128,4,128]{4,2,0,1,3:T(8,128)(2,1)}, u32[]{:S(2)}, u32[]{:S(2)}) async-start(bf16[16,1,128,4,128]{4,2,0,1,3:T(8,128)(2,1)} %copy.18), calls=%async_computation | async-start | bytes 4194304 | tf_op jit(solution)/shard_map/all_to_all | solution.py:47
  27.2 0.5 bitcast_convert_fusion.1
  27.6 1.3 copy.22
  29.0 0.5 bitcast_convert_fusion
  29.4 1.3 copy.23
  30.7 1.7 pad_maximum_fusion.1
  32.5 7.7 %copy.27 = bf16[512,16,2,64]{3,2,1,0:T(2,128)(2,1)} copy(bf16[512,16,2,64]{0,3,1,2:T(8,128)(2,1)S(1)} %pad_maximum_fusion.1) | data formatting | bytes 4194304 | tf_op jit(solution)/shard_map/reshape;reshape | solution.py:65
  40.1 7.8 %reshape.143 = bf16[8,64,16,128]{3,2,1,0:T(8,128)(2,1)} reshape(bf16[512,16,2,64]{3,2,1,0:T(2,128)(2,1)} %copy.27) | data formatting | bytes 4194304 | tf_op jit(solution)/shard_map/reshape;reshape | solution.py:65
  47.9 5.6 %all-to-all-done = bf16[16,1,128,4,128]{4,2,0,1,3:T(8,128)(2,1)} async-done(((bf16[16,1,128,4,128]{4,2,0,1,3:T(8,128)(2,1)}), bf16[16,1,128,4,128]{4,2,0,1,3:T(8,128)(2,1)}, u32[]{:S(2)}, u32[]{:S(2)}) %all-to-all-start) | async-done | bytes 2097184 | tf_op jit(solution)/shard_map/all_to_all | solution.py:47
  53.6 6.7 %all-to-all-start.2 = ((bf16[8,64,16,128]{3,2,1,0:T(8,128)(2,1)}), bf16[8,64,16,128]{3,2,1,0:T(8,128)(2,1)S(1)}, u32[]{:S(2)}, u32[]{:S(2)}) async-start(bf16[8,64,16,128]{3,2,1,0:T(8,128)(2,1)} %reshape.143), calls=%async_computation.2 | async-start | bytes 4194304 | tf_op jit(solution)/shard_map/all_to_all | solution.py:64
  60.2 1.7 copy.19
  62.0 1.5 copy.20
  63.5 44.8 %all-to-all-done.2 = bf16[8,64,16,128]{3,2,1,0:T(8,128)(2,1)S(1)} async-done(((bf16[8,64,16,128]{3,2,1,0:T(8,128)(2,1)}), bf16[8,64,16,128]{3,2,1,0:T(8,128)(2,1)S(1)}, u32[]{:S(2)}, u32[]{:S(2)}) %all-to-all-start.2) | async-done | bytes 2097184 | tf_op jit(solution)/shard_map/all_to_all | solution.py:64
  108.3 4.3 %all-to-all-start.1 = ((bf16[16,8,64,128]{3,2,0,1:T(8,128)(2,1)}), bf16[16,8,64,128]{3,2,0,1:T(8,128)(2,1)}, u32[]{:S(2)}, u32[]{:S(2)}) async-start(bf16[16,8,64,128]{3,2,0,1:T(8,128)(2,1)} %copy.20), calls=%async_computation.1 | async-start | bytes 4194304 | tf_op jit(solution)/shard_map/all_to_all | solution.py:56
  112.7 1.9 copy.26
  114.6 45.8 %all-to-all-done.1 = bf16[16,8,64,128]{3,2,0,1:T(8,128)(2,1)} async-done(((bf16[16,8,64,128]{3,2,0,1:T(8,128)(2,1)}), bf16[16,8,64,128]{3,2,0,1:T(8,128)(2,1)}, u32[]{:S(2)}, u32[]{:S(2)}) %all-to-all-start.1) | async-done | bytes 2097184 | tf_op jit(solution)/shard_map/all_to_all | solution.py:56
  160.4 3.1 %copy.21 = bf16[8,16,1,64,128]{4,1,0,3,2:T(8,128)(2,1)S(1)} copy(bf16[8,16,1,64,128]{4,3,1,0,2:T(8,128)(2,1)} %bitcast.15) | data formatting | bytes 4194304 | tf_op jit(solution)/shard_map/all_to_all | solution.py:56
  163.6 1.3 convolution_bitcast_fusion
  164.9 0.6 dynamic-slice
  166.2 58.3 %reduce-scatter.2.cloned.1.call-done = f32[16,128]{1,0:T(8,128)} async-done(((f32[128,128]{1,0:T(8,128)}), f32[16,128]{1,0:T(8,128)}) %reduce-scatter.2.cloned.1.call-update) | async-done | bytes 8208 | tf_op jit(solution)/shard_map/reduce_scatter | solution.py:75
  224.5 5.9 %all-reduce = f32[16,128]{1,0:T(8,128)S(1)} all-reduce(f32[16,128]{1,0:T(8,128)} %reduce-scatter.2.cloned.1.call-done), channel_id=3, replica_groups=mesh['grp'=8,'band'=4] {'band'}, use_global_device_ids=true, to_apply=%region_1.3.clone | all-reduce | flops 2048 | bytes 16384
  230.4 0.6 constant_dynamic-slice_fusion
  (23 shorter events, 1.2 us)
Async XLA Ops:
  6.5 6.3 %copy-start = (bf16[1,4,64,1024]{3,2,1,0:T(8,128)(2,1)S(1)}, bf16[1,4,64,1024]{3,2,1,0:T(8,128)(2,1)}, u32[]{:S(2)}) copy-start(bf16[1,4,64,1024]{3,2,1,0:T(8,128)(2,1)} %param.7) | copy-start | bytes 1572868
  6.5 4.6 %copy-start.2 = (bf16[512,512]{1,0:T(8,128)(2,1)S(1)}, bf16[512,512]{1,0:T(8,128)(2,1)}, u32[]{:S(2)}) copy-start(bf16[512,512]{1,0:T(8,128)(2,1)} %param.11) | copy-start | bytes 1572868
  22.7 30.9 %all-to-all-start = ((bf16[16,1,128,4,128]{4,2,0,1,3:T(8,128)(2,1)}), bf16[16,1,128,4,128]{4,2,0,1,3:T(8,128)(2,1)}, u32[]{:S(2)}, u32[]{:S(2)}) async-start(bf16[16,1,128,4,128]{4,2,0,1,3:T(8,128)(2,1)} %copy.18), calls=%async_computation | async-start | bytes 4194304 | tf_op jit(solution)/shard_map/all_to_all | solution.py:47
  53.6 54.7 %all-to-all-start.2 = ((bf16[8,64,16,128]{3,2,1,0:T(8,128)(2,1)}), bf16[8,64,16,128]{3,2,1,0:T(8,128)(2,1)S(1)}, u32[]{:S(2)}, u32[]{:S(2)}) async-start(bf16[8,64,16,128]{3,2,1,0:T(8,128)(2,1)} %reshape.143), calls=%async_computation.2 | async-start | bytes 4194304 | tf_op jit(solution)/shard_map/all_to_all | solution.py:64
  108.3 52.2 %all-to-all-start.1 = ((bf16[16,8,64,128]{3,2,0,1:T(8,128)(2,1)}), bf16[16,8,64,128]{3,2,0,1:T(8,128)(2,1)}, u32[]{:S(2)}, u32[]{:S(2)}) async-start(bf16[16,8,64,128]{3,2,0,1:T(8,128)(2,1)} %copy.20), calls=%async_computation.1 | async-start | bytes 4194304 | tf_op jit(solution)/shard_map/all_to_all | solution.py:56
  112.6 111.9 %reduce-scatter.2.cloned.1.call-start = ((), (), s32[]{:S(2)}) async-start(), calls=%async_computation.4 | async-start | bytes 73728 | tf_op jit(solution)/shard_map/reduce_scatter | solution.py:75
  160.4 3.1 %copy-start.1 = (bf16[1,64,8,16,128]{4,3,2,1,0:T(8,128)(2,1)S(1)}, bf16[1,64,8,16,128]{4,3,2,1,0:T(8,128)(2,1)}, u32[]{:S(2)}) copy-start(bf16[1,64,8,16,128]{4,3,2,1,0:T(8,128)(2,1)} %copy.26) | copy-start | bytes 6291460
  163.6 1.4 copy-start.3
Sparse Core Ops, SparseCore 0:
  165.0 59.4 reduce-scatter.1
where the time goes:
time: 239 us; the launch traced here: 238 us
  waiting for transfers between devices  155 us (65%)
  local copies, waits for them, and re-layouts  39.2 us (16%)
  starting transfers between devices  15.5 us (6%)
  between operations  15 us (6%)
  blocking collectives  5.87 us (2%)
  matrix products  4.12 us (2%)
  other arithmetic  3.53 us (1%)
    reduce_scatter x1, waiting for transfers between devices, on_device(): lax.psum_scatter(partial_value, 'grp', scatter_dimension=0, tiled=True)  58.3 us
    all_to_all x1, waiting for transfers between devices, on_device(): lax.all_to_all(moved.reshape(ri_local, group_count, pair_cols, band_orbs)...  45.8 us
    all_to_all x1, waiting for transfers between devices, on_device(): lax.all_to_all(virt_three.reshape(group_count, pair_cols, ri_local, band_...  44.8 us
    another operation x2, local copies, waits for them, and re-layouts, on_device(): virt_three.reshape(group_count, pair_cols, ri_local, band_orbs)  15.4 us
    all_to_all x1, starting transfers between devices, on_device(): lax.all_to_all(virt_three.reshape(group_count, pair_cols, ri_local, band_...  6.66 us
    unnamed x1, blocking collectives  5.87 us
    all_to_all x1, waiting for transfers between devices, on_device(): lax.all_to_all(occ_three.reshape(ri_local, 1, band_orbs, band_count, band...  5.64 us
    another operation x2, local copies, waits for them, and re-layouts, on_device(): occ_three.reshape(ri_local, 1, band_orbs, band_count, band_orbs)  5.53 us
  transfers between devices with their start and end apart: 4, of which 4 were waited for; matrix products, arithmetic and copies ran while one was open for 11% of the time, Pallas kernels for 0%

commit v1 on v0

--- a/solution.py
+++ b/solution.py
@@ -53,13 +53,19 @@
     )
     moved = moved.reshape(ri_local, orbitals, band_orbs)
     pair_cols = orbitals // group_count
-    occ_pairs = lax.all_to_all(
-        moved.reshape(ri_local, group_count, pair_cols, band_orbs),
-        "grp",
-        split_axis=1,
-        concat_axis=0,
-        tiled=True,
-    )
+    value = moved.reshape(ri_local, group_count, pair_cols, band_orbs)
+    ways, here = (lax.axis_size("grp"), lax.axis_index("grp"))
+    width = value.shape[1] // ways
+    shape = list(value.shape)
+    shape[1] = width
+    height = shape[0]
+    shape[0] = height * ways
+    occ_pairs = jnp.zeros(shape, value.dtype)
+    for mask in range(ways):
+        part = lax.dynamic_slice_in_dim(value, (here ^ mask) * width, width, axis=1)
+        if mask:
+            part = lax.ppermute(part, "grp", [(d, d ^ mask) for d in range(ways)])
+        occ_pairs = lax.dynamic_update_slice_in_dim(occ_pairs, part, (here ^ mask) * height, axis=0)
     occ_pairs = occ_pairs.reshape(ri_total, pair_cols, band_orbs)
     virt_pairs = lax.all_to_all(
         virt_three.reshape(group_count, pair_cols, ri_local, band_orbs),

time: 239 us -> 231 us (0.967)
  waiting for transfers between devices: 155 us -> 128 us
  starting transfers between devices: 15.5 us -> 28.2 us
  local copies, waits for them, and re-layouts: 39.2 us -> 44.5 us
    ppermute x0 -> x7, waiting for transfers between devices: none -> 56.5 us  [on_device(): part = lax.ppermute(part, 'grp', [(d, d ^ mask) for d in range(ways)])]
    all_to_all x1 -> x0, waiting for transfers between devices: 45.8 us -> none  [on_device(): lax.all_to_all(moved.reshape(ri_local, group_count, pair_cols, band_orbs)...]
    all_to_all x1, waiting for transfers between devices: 44.8 us -> 0.01 us  [on_device(): lax.all_to_all(virt_three.reshape(group_count, pair_cols, ri_local, band_...]
    ppermute x0 -> x7, starting transfers between devices: none -> 17 us  [on_device(): part = lax.ppermute(part, 'grp', [(d, d ^ mask) for d in range(ways)])]
    dynamic_update_slice x0 -> x8, local copies, waits for them, and re-layouts: none -> 8.22 us  [on_device(): lax.dynamic_update_slice_in_dim(occ_pairs, part, (here ^ mask) * height,...]
    reduce_scatter x1, waiting for transfers between devices: 58.3 us -> 65.7 us  [on_device(): lax.psum_scatter(partial_value, 'grp', scatter_dimension=0, tiled=True)]
    all_to_all x1 -> x0, starting transfers between devices: 4.35 us -> none  [on_device(): lax.all_to_all(moved.reshape(ri_local, group_count, pair_cols, band_orbs)...]
    all_to_all x1 -> x0, local copies, waits for them, and re-layouts: 3.09 us -> none  [on_device(): lax.all_to_all(moved.reshape(ri_local, group_count, pair_cols, band_orbs)...]
  transfers between devices with their start and end apart: 4 -> 10, of which waited for: 4 -> 7; matrix products, arithmetic and copies ran while one was open for 11% -> 15% of each run, Pallas kernels for 0% -> 0%
where the time goes in v1:
time: 231 us
  waiting for transfers between devices  128 us (55%)
  local copies, waits for them, and re-layouts  44.5 us (19%)
  starting transfers between devices  28.2 us (12%)
  between operations  15 us (6%)
  blocking collectives  5.87 us (3%)
  matrix products  5.75 us (2%)
  other arithmetic  3.53 us (2%)
    reduce_scatter x1, waiting for transfers between devices, on_device(): lax.psum_scatter(partial_value, 'grp', scatter_dimension=0, tiled=True)  65.7 us
    ppermute x7, waiting for transfers between devices, on_device(): part = lax.ppermute(part, 'grp', [(d, d ^ mask) for d in range(ways)])  56.5 us
    ppermute x7, starting transfers between devices, on_device(): part = lax.ppermute(part, 'grp', [(d, d ^ mask) for d in range(ways)])  17 us
    another operation x2, local copies, waits for them, and re-layouts, on_device(): virt_three.reshape(group_count, pair_cols, ri_local, band_orbs)  15.5 us
    dynamic_update_slice x8, local copies, waits for them, and re-layouts, on_device(): lax.dynamic_update_slice_in_dim(occ_pairs, part, (here ^ mask) * height,...  8.22 us
    all_to_all x1, starting transfers between devices, on_device(): lax.all_to_all(virt_three.reshape(group_count, pair_cols, ri_local, band_...  6.7 us
    unnamed x1, blocking collectives  5.87 us
    all_to_all x1, waiting for transfers between devices, on_device(): lax.all_to_all(occ_three.reshape(ri_local, 1, band_orbs, band_count, band...  5.54 us
  transfers between devices with their start and end apart: 10, of which 7 were waited for; matrix products, arithmetic and copies ran while one was open for 15% of the time, Pallas kernels for 0%

profile of v1, /device:TPU:0, one launch (start us, length us, event | category | flops | bytes accessed | tf_op | source)
XLA Modules:
  0.0 230.5 jit_solution(2056220244586961029)
XLA Ops:
  8.8 2.3 %gather_fusion = bf16[256,512]{1,0:T(8,128)(2,1)S(1)} fusion(bf16[512,512]{1,0:T(8,128)(2,1)} %param.10, s32[1024]{0:T(1024)S(1)} %pad_clamp_fusion), kind=kCustom, calls=%fused_computation.clone | custom fusion | bytes 525312 | tf_op jit(solution)/shard_map/jit(_take)/gather | solution.py:26
  11.1 1.2 gather_fusion.1
  13.8 1.4 fusion
  15.3 1.5 copy.44
  17.2 2.1 reshape_reshape.9
  19.3 3.5 %copy.47 = bf16[16,1,128,4,128]{4,2,0,1,3:T(8,128)(2,1)} copy(bf16[16,1,128,4,128]{4,3,2,0,1:T(4,128)(2,1)} %reshape_reshape.9) | data formatting | bytes 4194304 | tf_op jit(solution)/shard_map/reshape;reshape | solution.py:48
  22.7 4.5 %all-to-all-start = ((bf16[16,1,128,4,128]{4,2,0,1,3:T(8,128)(2,1)}), bf16[16,1,128,4,128]{4,2,0,1,3:T(8,128)(2,1)}, u32[]{:S(2)}, u32[]{:S(2)}) async-start(bf16[16,1,128,4,128]{4,2,0,1,3:T(8,128)(2,1)} %copy.47), calls=%async_computation | async-start | bytes 4194304 | tf_op jit(solution)/shard_map/all_to_all | solution.py:47
  27.7 1.3 copy.57
  29.5 1.3 copy.58
  30.8 1.7 pad_maximum_fusion.1
  32.5 7.7 %copy.62 = bf16[512,16,2,64]{3,2,1,0:T(2,128)(2,1)} copy(bf16[512,16,2,64]{0,3,1,2:T(8,128)(2,1)S(1)} %pad_maximum_fusion.1) | data formatting | bytes 4194304 | tf_op jit(solution)/shard_map/reshape;reshape | solution.py:71
  40.2 7.8 %reshape.182 = bf16[8,64,16,128]{3,2,1,0:T(8,128)(2,1)} reshape(bf16[512,16,2,64]{3,2,1,0:T(2,128)(2,1)} %copy.62) | data formatting | bytes 4194304 | tf_op jit(solution)/shard_map/reshape;reshape | solution.py:71
  48.0 5.5 %all-to-all-done = bf16[16,1,128,4,128]{4,2,0,1,3:T(8,128)(2,1)} async-done(((bf16[16,1,128,4,128]{4,2,0,1,3:T(8,128)(2,1)}), bf16[16,1,128,4,128]{4,2,0,1,3:T(8,128)(2,1)}, u32[]{:S(2)}, u32[]{:S(2)}) %all-to-all-start) | async-done | bytes 2097184 | tf_op jit(solution)/shard_map/all_to_all | solution.py:47
  53.5 6.7 %all-to-all-start.1 = ((bf16[8,64,16,128]{3,2,1,0:T(8,128)(2,1)}), bf16[8,64,16,128]{3,2,1,0:T(8,128)(2,1)S(1)}, u32[]{:S(2)}, u32[]{:S(2)}) async-start(bf16[8,64,16,128]{3,2,1,0:T(8,128)(2,1)} %reshape.182), calls=%async_computation.1 | async-start | bytes 4194304 | tf_op jit(solution)/shard_map/all_to_all | solution.py:70
  60.3 1.7 copy.48
  62.1 1.1 constant_dynamic-slice_fusion
  63.2 1.9 collective-permute-start
  65.1 1.5 collective-permute-start.1
  66.7 2.8 %collective-permute-start.3 = (bf16[16,1,64,128]{3,2,1,0:T(8,128)(2,1)}, bf16[16,1,64,128]{3,2,1,0:T(8,128)(2,1)S(1)}, u32[]{:S(2)}, u32[]{:S(2)}) collective-permute-start(bf16[16,1,64,128]{3,2,1,0:T(8,128)(2,1)} %get-tuple-element.11), channel_id=1, source_target_pairs={{0,16},{4,20},{8,24},{12,28},{16,0},{20,4},{24,8},{28,12},{1,17},{... | collective-permute-start | bytes 786440 | tf_op jit(solution)/shard_map/ppermute | solution.py:67
  69.5 1.5 collective-permute-start.4
  70.9 1.8 reshape.141
  73.7 10.4 %collective-permute-done = bf16[16,1,64,128]{3,2,1,0:T(8,128)(2,1)} collective-permute-done((bf16[16,1,64,128]{3,2,1,0:T(8,128)(2,1)}, bf16[16,1,64,128]{3,2,1,0:T(8,128)(2,1)}, u32[]{:S(2)}, u32[]{:S(2)}) %collective-permute-start) | collective-permute-done | bytes 262176 | tf_op jit(solution)/shard_map/ppermute | solution.py:67
  84.1 5.4 %collective-permute-start.5 = (bf16[16,1,64,128]{3,2,1,0:T(8,128)(2,1)S(1)}, bf16[16,1,64,128]{3,2,1,0:T(8,128)(2,1)S(1)}, u32[]{:S(2)}, u32[]{:S(2)}) collective-permute-start(bf16[16,1,64,128]{3,2,1,0:T(8,128)(2,1)S(1)} %get-tuple-element.9), channel_id=1, source_target_pairs={{0,24},{4,28},{8,16},{12,20},{16,8},{20,12},{24,0},{28,4},{1,25},{... | collective-permute-start | bytes 786440 | tf_op jit(solution)/shard_map/ppermute | solution.py:67
  89.5 1.8 copy_dynamic-update-slice_fusion.6
  91.3 10.7 %collective-permute-done.1 = bf16[16,1,64,128]{3,2,1,0:T(8,128)(2,1)S(1)} collective-permute-done((bf16[16,1,64,128]{3,2,1,0:T(8,128)(2,1)}, bf16[16,1,64,128]{3,2,1,0:T(8,128)(2,1)S(1)}, u32[]{:S(2)}, u32[]{:S(2)}) %collective-permute-start.1) | collective-permute-done | bytes 262176 | tf_op jit(solution)/shard_map/ppermute | solution.py:67
  102.0 3.8 %collective-permute-start.6 = (bf16[16,1,64,128]{3,2,1,0:T(8,128)(2,1)S(1)}, bf16[16,1,64,128]{3,2,1,0:T(8,128)(2,1)S(1)}, u32[]{:S(2)}, u32[]{:S(2)}) collective-permute-start(bf16[16,1,64,128]{3,2,1,0:T(8,128)(2,1)S(1)} %get-tuple-element.8), channel_id=1, source_target_pairs={{0,28},{4,24},{8,20},{12,16},{16,12},{20,8},{24,4},{28,0},{1,29},{... | collective-permute-start | bytes 786440 | tf_op jit(solution)/shard_map/ppermute | solution.py:67
  108.5 29.5 %collective-permute-done.3 = bf16[16,1,64,128]{3,2,1,0:T(8,128)(2,1)S(1)} collective-permute-done((bf16[16,1,64,128]{3,2,1,0:T(8,128)(2,1)}, bf16[16,1,64,128]{3,2,1,0:T(8,128)(2,1)S(1)}, u32[]{:S(2)}, u32[]{:S(2)}) %collective-permute-start.3) | collective-permute-done | bytes 262176 | tf_op jit(solution)/shard_map/ppermute | solution.py:67
  138.9 5.0 %collective-permute-done.4 = bf16[16,1,64,128]{3,2,1,0:T(8,128)(2,1)S(1)} collective-permute-done((bf16[16,1,64,128]{3,2,1,0:T(8,128)(2,1)}, bf16[16,1,64,128]{3,2,1,0:T(8,128)(2,1)S(1)}, u32[]{:S(2)}, u32[]{:S(2)}) %collective-permute-start.4) | collective-permute-done | bytes 262176 | tf_op jit(solution)/shard_map/ppermute | solution.py:67
  144.0 0.9 copy_dynamic-update-slice_fusion.2
  147.3 2.9 %convolution_bitcast_fusion = f32[128,128]{1,0:T(8,128)} fusion(bf16[128,64,128]{2,0,1:T(8,128)(2,1)} %copy_dynamic-update-slice_fusion, bf16[64,128,128]{2,1,0:T(8,128)(2,1)S(1)} %bitcast.81), kind=kOutput, calls=%fused_computation.10 | convolution fusion | flops 268435456 | bytes 4259840 | tf_op jit(solution)/shard_map/dot_general | solution.py:78
  151.5 65.7 %reduce-scatter.2.cloned.1.call-done = f32[16,128]{1,0:T(8,128)} async-done(((f32[128,128]{1,0:T(8,128)}), f32[16,128]{1,0:T(8,128)}) %reduce-scatter.2.cloned.1.call-update) | async-done | bytes 8208 | tf_op jit(solution)/shard_map/reduce_scatter | solution.py:81
  217.2 5.9 %all-reduce = f32[16,128]{1,0:T(8,128)S(1)} all-reduce(f32[16,128]{1,0:T(8,128)} %reduce-scatter.2.cloned.1.call-done), channel_id=3, replica_groups=mesh['grp'=8,'band'=4] {'band'}, use_global_device_ids=true, to_apply=%region_1.3.clone | all-reduce | flops 2048 | bytes 16384
  (41 shorter events, 12.6 us)
Async XLA Ops:
  6.5 6.3 %copy-start = (bf16[1,4,64,1024]{3,2,1,0:T(8,128)(2,1)S(1)}, bf16[1,4,64,1024]{3,2,1,0:T(8,128)(2,1)}, u32[]{:S(2)}) copy-start(bf16[1,4,64,1024]{3,2,1,0:T(8,128)(2,1)} %param.7) | copy-start | bytes 1572868
  6.5 4.6 %copy-start.1 = (bf16[512,512]{1,0:T(8,128)(2,1)S(1)}, bf16[512,512]{1,0:T(8,128)(2,1)}, u32[]{:S(2)}) copy-start(bf16[512,512]{1,0:T(8,128)(2,1)} %param.11) | copy-start | bytes 1572868
  22.7 30.8 %all-to-all-start = ((bf16[16,1,128,4,128]{4,2,0,1,3:T(8,128)(2,1)}), bf16[16,1,128,4,128]{4,2,0,1,3:T(8,128)(2,1)}, u32[]{:S(2)}, u32[]{:S(2)}) async-start(bf16[16,1,128,4,128]{4,2,0,1,3:T(8,128)(2,1)} %copy.47), calls=%async_computation | async-start | bytes 4194304 | tf_op jit(solution)/shard_map/all_to_all | solution.py:47
  53.5 93.1 %all-to-all-start.1 = ((bf16[8,64,16,128]{3,2,1,0:T(8,128)(2,1)}), bf16[8,64,16,128]{3,2,1,0:T(8,128)(2,1)S(1)}, u32[]{:S(2)}, u32[]{:S(2)}) async-start(bf16[8,64,16,128]{3,2,1,0:T(8,128)(2,1)} %reshape.182), calls=%async_computation.1 | async-start | bytes 4194304 | tf_op jit(solution)/shard_map/all_to_all | solution.py:70
  60.2 157.0 %reduce-scatter.2.cloned.1.call-start = ((), (), s32[]{:S(2)}) async-start(), calls=%async_computation.3 | async-start | bytes 73728 | tf_op jit(solution)/shard_map/reduce_scatter | solution.py:81
  63.2 20.9 %collective-permute-start = (bf16[16,1,64,128]{3,2,1,0:T(8,128)(2,1)}, bf16[16,1,64,128]{3,2,1,0:T(8,128)(2,1)}, u32[]{:S(2)}, u32[]{:S(2)}) collective-permute-start(bf16[16,1,64,128]{3,2,1,0:T(8,128)(2,1)} %get-tuple-element.14), channel_id=1, source_target_pairs={{0,4},{4,0},{8,12},{12,8},{16,20},{20,16},{24,28},{28,24},{1,5},{5... | collective-permute-start | bytes 786440 | tf_op jit(solution)/shard_map/ppermute | solution.py:67
  65.1 36.9 %collective-permute-start.1 = (bf16[16,1,64,128]{3,2,1,0:T(8,128)(2,1)}, bf16[16,1,64,128]{3,2,1,0:T(8,128)(2,1)S(1)}, u32[]{:S(2)}, u32[]{:S(2)}) collective-permute-start(bf16[16,1,64,128]{3,2,1,0:T(8,128)(2,1)} %get-tuple-element.13), channel_id=1, source_target_pairs={{0,8},{4,12},{8,0},{12,4},{16,24},{20,28},{24,16},{28,20},{1,9},{5... | collective-permute-start | bytes 786440 | tf_op jit(solution)/shard_map/ppermute | solution.py:67
  66.6 41.1 %collective-permute-start.2 = (bf16[16,1,64,128]{3,2,1,0:T(8,128)(2,1)}, bf16[16,1,64,128]{3,2,1,0:T(8,128)(2,1)S(1)}, u32[]{:S(2)}, u32[]{:S(2)}) collective-permute-start(bf16[16,1,64,128]{3,2,1,0:T(8,128)(2,1)} %get-tuple-element.12), channel_id=1, source_target_pairs={{0,12},{4,8},{8,4},{12,0},{16,28},{20,24},{24,20},{28,16},{1,13},{... | collective-permute-start | bytes 786440 | tf_op jit(solution)/shard_map/ppermute | solution.py:67
  66.7 71.3 %collective-permute-start.3 = (bf16[16,1,64,128]{3,2,1,0:T(8,128)(2,1)}, bf16[16,1,64,128]{3,2,1,0:T(8,128)(2,1)S(1)}, u32[]{:S(2)}, u32[]{:S(2)}) collective-permute-start(bf16[16,1,64,128]{3,2,1,0:T(8,128)(2,1)} %get-tuple-element.11), channel_id=1, source_target_pairs={{0,16},{4,20},{8,24},{12,28},{16,0},{20,4},{24,8},{28,12},{1,17},{... | collective-permute-start | bytes 786440 | tf_op jit(solution)/shard_map/ppermute | solution.py:67
  69.5 74.5 %collective-permute-start.4 = (bf16[16,1,64,128]{3,2,1,0:T(8,128)(2,1)}, bf16[16,1,64,128]{3,2,1,0:T(8,128)(2,1)S(1)}, u32[]{:S(2)}, u32[]{:S(2)}) collective-permute-start(bf16[16,1,64,128]{3,2,1,0:T(8,128)(2,1)} %get-tuple-element.10), channel_id=1, source_target_pairs={{0,20},{4,16},{8,28},{12,24},{16,4},{20,0},{24,12},{28,8},{1,21},{... | collective-permute-start | bytes 786440 | tf_op jit(solution)/shard_map/ppermute | solution.py:67
  84.1 60.8 %collective-permute-start.5 = (bf16[16,1,64,128]{3,2,1,0:T(8,128)(2,1)S(1)}, bf16[16,1,64,128]{3,2,1,0:T(8,128)(2,1)S(1)}, u32[]{:S(2)}, u32[]{:S(2)}) collective-permute-start(bf16[16,1,64,128]{3,2,1,0:T(8,128)(2,1)S(1)} %get-tuple-element.9), channel_id=1, source_target_pairs={{0,24},{4,28},{8,16},{12,20},{16,8},{20,12},{24,0},{28,4},{1,25},{... | collective-permute-start | bytes 786440 | tf_op jit(solution)/shard_map/ppermute | solution.py:67
  102.0 43.8 %collective-permute-start.6 = (bf16[16,1,64,128]{3,2,1,0:T(8,128)(2,1)S(1)}, bf16[16,1,64,128]{3,2,1,0:T(8,128)(2,1)S(1)}, u32[]{:S(2)}, u32[]{:S(2)}) collective-permute-start(bf16[16,1,64,128]{3,2,1,0:T(8,128)(2,1)S(1)} %get-tuple-element.8), channel_id=1, source_target_pairs={{0,28},{4,24},{8,20},{12,16},{16,12},{20,8},{24,4},{28,0},{1,29},{... | collective-permute-start | bytes 786440 | tf_op jit(solution)/shard_map/ppermute | solution.py:67
  147.3 3.0 %copy-start.2 = (u32[32]{0:T(128)S(1)}, u32[32]{0:T(128)}, u32[]{:S(2)}) copy-start(u32[32]{0:T(128)} %constant.79) | copy-start | bytes 388
Sparse Core Ops, SparseCore 0:
  150.4 66.7 reduce-scatter.1
